TPU v7x, 128 devices: a whole 4x4x4 slice. The times are simulated.
128 devices in a mesh: seq: 32 (over z, x, y_lo), type: 4 (over y_hi, core).
Axes of the slice: x: 4, y: 4 (y_hi: 2, y_lo: 2; y = y_hi * 2 + y_lo), z: 4, core: 2. Of those that a mesh axis runs over, the one named last changes fastest.
Arguments:
- tokens: bfloat16 [17408, 1024], P(('seq', 'type')), may hold values from -60 to 60
- shift_scale: float32 [2, 1024], replicated, may hold values from -0.8 to 0.8
- branch_gate: float32 [1024], replicated, may hold values from 0.25 to 1.75
- final_gain: float32 [1024], replicated, may hold values from 0.5 to 1.5
- w_qkv: bfloat16 [3, 1024, 1024], P(None, None, 'type'), may hold values from -1 to 1
- w_out: bfloat16 [1024, 1024], P('type'), may hold values from -0.375 to 0.375
- type_ids: int32 [17408, 1], P(('seq', 'type')), may hold values from 0 to 7; in each aligned block of 136 rows (0 to 135, 136 to 271, ...) at most 51 rows name the same one
- head_w1: bfloat16 [8, 1024, 1024], P('type'), may hold values from -0.1875 to 0.1875
- head_b1: bfloat16 [8, 1024], P('type'), may hold values from -3 to 3
- head_w2: bfloat16 [8, 1024, 16], P('type'), may hold values from -0.1875 to 0.1875
Outputs:
- updated: bfloat16 [17408, 1024], P(('seq', 'type'))
- head_out: float32 [17408, 16], P(('seq', 'type'))
Inputs may be any that keep to these rules, and one draw needn't show every extreme that they name: `type_ids`: among the 136 tokens of one device no type occurs more than 51 times; some type occurs exactly 51 times on some devices.
All inputs are finite; a program needn't handle non-finite values.
Results may differ from a plain program's by a relative error of at most 0.014.
Values may be sent and summed in bfloat16 or wider, within the bound.
No kernel may reach another device: no remote copies, remote signals or barrier semaphores. Data moves between devices by JAX's collectives and lax.ppermute only.
A program may use at most 192 MiB of HBM per device.

v0:
```python
import jax
import jax.numpy as jnp
from jax import lax
from jax.sharding import PartitionSpec as P

HD = 64


def rms_normalize(values):
    squares = jnp.mean(values * values, axis=-1, keepdims=True)
    return values * lax.rsqrt(squares + 1e-06)


def absorb_block(state, query_heads, key_heads, value_heads):
    largest, totals, numer = state
    scores = jnp.einsum(
        "qhd,khd->hqk", query_heads, key_heads, preferred_element_type=jnp.float32
    ) * HD ** (-0.5)
    newmax = jnp.maximum(largest, jnp.max(scores, axis=-1))
    decay = jnp.exp(largest - newmax)
    weights = jnp.exp(scores - newmax[:, :, None])
    totals = totals * decay + jnp.sum(weights, axis=-1)
    update = jnp.einsum(
        "hqk,khd->qhd",
        weights.astype(jnp.bfloat16),
        value_heads,
        preferred_element_type=jnp.float32,
    )
    numer = numer * jnp.transpose(decay)[:, :, None] + update
    return (newmax, totals, numer)


def apply_heads(feature_slots, first_w, first_b, second_w):
    hidden = jnp.einsum(
        "...tcd,tdh->...tch", feature_slots, first_w, preferred_element_type=jnp.float32
    )
    hidden = jax.nn.gelu(hidden + first_b.astype(jnp.float32)[:, None, :]).astype(jnp.bfloat16)
    return jnp.einsum("...tch,tho->...tco", hidden, second_w, preferred_element_type=jnp.float32)


def body(
    tokens, shift_scale, branch_gate, final_gain, w_qkv, w_out, type_ids, head_w1, head_b1, head_w2
):
    inputs = tokens.astype(jnp.float32)
    modulated = (rms_normalize(inputs) * (1.0 + shift_scale[1]) + shift_scale[0]).astype(
        jnp.bfloat16
    )
    projected = jnp.einsum(
        "rd,ide->ire",
        lax.all_gather(modulated, "type", axis=0, tiled=True),
        w_qkv,
        preferred_element_type=jnp.float32,
    ).astype(jnp.bfloat16)
    queries = projected[0]
    local_keys = projected[1]
    local_values = projected[2]
    query_count = queries.shape[0]
    width = queries.shape[1]
    local_heads = width // HD
    query_heads = queries.reshape(query_count, local_heads, HD)
    initial = (
        jnp.full((local_heads, query_count), -1e30, jnp.float32),
        jnp.zeros((local_heads, query_count), jnp.float32),
        jnp.zeros((query_count, local_heads, HD), jnp.float32),
    )
    running = initial
    key_part = lax.all_gather(local_keys, "seq", axis=0, tiled=True)
    value_part = lax.all_gather(local_values, "seq", axis=0, tiled=True)
    row_total = key_part.shape[0]
    key_blocks = key_part.reshape(row_total // 512, 512, local_heads, HD)
    value_blocks = value_part.reshape(row_total // 512, 512, local_heads, HD)

    def advance(state, pair):
        return (absorb_block(state, query_heads, pair[0], pair[1]), None)

    running, unused = lax.scan(advance, running, (key_blocks, value_blocks))
    largest, totals, numer = running
    attended = (
        (numer / jnp.transpose(totals)[:, :, None]).astype(jnp.bfloat16).reshape(query_count, width)
    )
    mixed = lax.psum_scatter(
        jnp.dot(attended, w_out, preferred_element_type=jnp.float32),
        "type",
        scatter_dimension=0,
        tiled=True,
    )
    updated = (inputs + branch_gate * mixed).astype(jnp.bfloat16)
    final = (rms_normalize(updated.astype(jnp.float32)) * final_gain).astype(jnp.bfloat16)
    owned = head_w1.shape[0]
    owners = lax.axis_size("type")
    kinds_all = owned * owners
    capacity = 3 * tokens.shape[0] // 8
    kinds = type_ids[:, 0]
    onehot = (kinds[:, None] == jnp.arange(kinds_all, dtype=jnp.int32)[None, :]).astype(jnp.int32)
    ranks = jnp.sum((jnp.cumsum(onehot, axis=0) - onehot) * onehot, axis=1)
    slots = kinds * capacity + ranks
    slot_ids = jnp.arange(kinds_all * capacity, dtype=jnp.int32)
    dispatch = (slot_ids[:, None] == slots[None, :]).astype(jnp.bfloat16)
    packed = jnp.dot(dispatch, final, preferred_element_type=jnp.float32).astype(jnp.bfloat16)
    packed = packed.reshape(kinds_all, capacity, final.shape[1])
    first_w, first_b, second_w = (
        lax.all_gather(head_w1, "type", axis=0, tiled=True),
        lax.all_gather(head_b1, "type", axis=0, tiled=True),
        lax.all_gather(head_w2, "type", axis=0, tiled=True),
    )
    answers = apply_heads(packed, first_w, first_b, second_w)
    answers = answers.reshape(kinds_all * capacity, head_w2.shape[2])
    gather_back = (slots[:, None] == slot_ids[None, :]).astype(jnp.float32)
    head_out = jnp.dot(
        gather_back, answers, precision=lax.Precision.HIGHEST, preferred_element_type=jnp.float32
    )
    return (updated, head_out)


def solution(mesh):
    in_specs = (
        P(("seq", "type"), None),
        P(),
        P(),
        P(),
        P(None, None, "type"),
        P("type", None),
        P(("seq", "type"), None),
        P("type", None, None),
        P("type", None),
        P("type", None, None),
    )
    out_specs = (P(("seq", "type"), None), P(("seq", "type"), None))
    return jax.shard_map(body, mesh=mesh, in_specs=in_specs, out_specs=out_specs, check_vma=False)
```

profile of v0, /device:TPU:1, one launch (start us, length us, event | category | flops | bytes accessed | tf_op | source)
XLA Modules:
  0.0 957.8 jit_solution(635125774649194052)
XLA Ops:
  11.1 24.9 %all-gather.8.cloned.1.call-done = bf16[544,1024]{1,0:T(8,128)(2,1)} async-done(((bf16[136,1024]{1,0:T(8,128)(2,1)}), bf16[544,1024]{1,0:T(8,128)(2,1)}) %all-gather.8.cloned.1.call-update) | async-done | bytes 1114128 | tf_op jit(solution)/shard_map/all_gather | solution.py:50
  40.1 196.5 %all-gather.12.cloned.1.call-done = bf16[1,17408,256]{2,1,0:T(8,128)(2,1)} async-done(((bf16[1,544,256]{2,1,0:T(8,128)(2,1)}), bf16[1,17408,256]{2,1,0:T(8,128)(2,1)}) %all-gather.12.cloned.1.call-update) | async-done | bytes 8912912 | tf_op jit(solution)/shard_map/all_gather | solution.py:67
  236.6 25.9 %reshape.77 = bf16[34,512,4,64]{3,2,1,0:T(4,128)(2,1)} reshape(bf16[1,17408,256]{2,1,0:T(8,128)(2,1)} %all-gather.12.cloned.1.call-done) | data formatting | bytes 17825792 | tf_op jit(solution)/shard_map/reshape | solution.py:70
  262.5 25.6 %copy.24 = bf16[34,512,4,64]{1,3,2,0:T(8,128)(2,1)} copy(bf16[34,512,4,64]{3,2,1,0:T(4,128)(2,1)} %reshape.77) | data formatting | bytes 17825792
  288.2 150.6 %all-gather.14.cloned.1.call-done = bf16[1,17408,256]{2,1,0:T(8,128)(2,1)} async-done(((bf16[1,544,256]{2,1,0:T(8,128)(2,1)}), bf16[1,17408,256]{2,1,0:T(8,128)(2,1)}) %all-gather.14.cloned.1.call-update) | async-done | bytes 8912912 | tf_op jit(solution)/shard_map/all_gather | solution.py:68
  438.8 25.9 %reshape.78 = bf16[34,512,4,64]{3,2,1,0:T(4,128)(2,1)} reshape(bf16[1,17408,256]{2,1,0:T(8,128)(2,1)} %all-gather.14.cloned.1.call-done) | data formatting | bytes 17825792 | tf_op jit(solution)/shard_map/reshape | solution.py:71
  464.7 25.6 %copy.25 = bf16[34,512,4,64]{1,3,2,0:T(8,128)(2,1)} copy(bf16[34,512,4,64]{3,2,1,0:T(4,128)(2,1)} %reshape.78) | data formatting | bytes 17825792
  490.3 298.6 %while.15 = (s32[]{:T(128)}, f32[4,544]{1,0:T(4,128)S(1)}, f32[4,544]{1,0:T(4,128)S(1)}, f32[544,4,64]{0,2,1:T(8,128)S(1)}, bf16[34,512,4,64]{1,3,2,0:T(8,128)(2...) while((s32[]{:T(128)}, f32[4,544]{1,0:T(4,128)S(1)}, ...), condition=%wide.region_4.5_spmd.clone, body=%wide.region_1.4_spmd.clone.sunk | while | flops 294556416 | bytes 33252484 | solution.py:76
  490.3 3.8 bitcast_reduce_fusion.2
  499.2 3.8 bitcast_reduce_fusion.2
  503.0 3.6 fusion.83
  507.9 3.8 bitcast_reduce_fusion.2
  511.7 3.6 fusion.83
  516.7 3.8 bitcast_reduce_fusion.2
  520.5 3.6 fusion.83
  525.5 3.8 bitcast_reduce_fusion.2
  534.3 3.8 bitcast_reduce_fusion.2
  543.1 3.8 bitcast_reduce_fusion.2
  546.9 3.6 fusion.83
  551.9 3.8 bitcast_reduce_fusion.2
  555.6 3.6 fusion.83
  560.6 3.8 bitcast_reduce_fusion.2
  564.4 3.6 fusion.83
  569.4 3.8 bitcast_reduce_fusion.2
  578.2 3.8 bitcast_reduce_fusion.2
  587.0 3.8 bitcast_reduce_fusion.2
  595.8 3.8 bitcast_reduce_fusion.2
  599.5 3.6 fusion.83
  604.5 3.8 bitcast_reduce_fusion.2
  608.3 3.6 fusion.83
  613.3 3.8 bitcast_reduce_fusion.2
  622.1 3.8 bitcast_reduce_fusion.2
  630.9 3.8 bitcast_reduce_fusion.2
  639.7 3.8 bitcast_reduce_fusion.2
  643.5 3.6 fusion.83
  648.4 3.8 bitcast_reduce_fusion.2
  652.2 3.6 fusion.83
  657.2 3.8 bitcast_reduce_fusion.2
  666.0 3.8 bitcast_reduce_fusion.2
  674.8 3.8 bitcast_reduce_fusion.2
  683.6 3.8 bitcast_reduce_fusion.2
  687.4 3.6 fusion.83
  692.4 3.8 bitcast_reduce_fusion.2
  696.1 3.6 fusion.83
  701.1 3.8 bitcast_reduce_fusion.2
  709.9 3.8 bitcast_reduce_fusion.2
  718.7 3.8 bitcast_reduce_fusion.2
  722.5 3.6 fusion.83
  727.5 3.8 bitcast_reduce_fusion.2
  731.3 3.6 fusion.83
  736.3 3.8 bitcast_reduce_fusion.2
  740.1 3.6 fusion.83
  745.0 3.8 bitcast_reduce_fusion.2
  753.8 3.8 bitcast_reduce_fusion.2
  762.6 3.8 bitcast_reduce_fusion.2
  771.4 3.8 bitcast_reduce_fusion.2
  775.2 3.6 fusion.83
  780.2 3.8 bitcast_reduce_fusion.2
  784.0 3.6 fusion.83
  792.4 11.0 %all-gather.2 = bf16[4,2,1024]{2,1,0:T(2,128)(2,1)S(1)} all-gather(bf16[1,2,1024]{2,1,0:T(2,128)(2,1)S(1)} %bitcast.83), channel_id=1, replica_groups=mesh['seq'=32,'type'=4] {'type'}, dimensions={0}, use_global_device_ids=true | all-gather | bytes 20480 | tf_op jit(solution)/shard_map/all_gather | solution.py:103
  803.5 7.4 all_gather.23
  811.0 20.2 %reduce-scatter.2.cloned.1.call-done = f32[136,1024]{1,0:T(8,128)} async-done(((f32[544,1024]{1,0:T(8,128)}), f32[136,1024]{1,0:T(8,128)}) %reduce-scatter.2.cloned.1.call-update) | async-done | bytes 557072 | tf_op jit(solution)/shard_map/reduce_scatter | solution.py:81
  833.3 109.4 %all-gather.10.cloned.1.call-done = bf16[8,1024,1024]{2,1,0:T(8,128)(2,1)} async-done(((bf16[2,1024,1024]{2,1,0:T(8,128)(2,1)}), bf16[8,1024,1024]{2,1,0:T(8,128)(2,1)}) %all-gather.10.cloned.1.call-update) | async-done | bytes 16777232 | tf_op jit(solution)/shard_map/all_gather | solution.py:102
  942.7 7.6 fusion.32
  (281 shorter events, 122.0 us)
Async XLA Ops:
  7.2 28.8 %copy-start = (bf16[3,1024,256]{2,1,0:T(8,128)(2,1)S(1)}, bf16[3,1024,256]{2,1,0:T(8,128)(2,1)}, u32[]{:S(2)}) copy-start(bf16[3,1024,256]{2,1,0:T(8,128)(2,1)} %param.16) | copy-start | bytes 4718596
  7.2 28.7 %all-gather.8.cloned.1.call-start = ((), (), s32[]{:S(2)}) async-start(), calls=%async_computation.1 | async-start | bytes 1392640 | tf_op jit(solution)/shard_map/all_gather | solution.py:50
  11.0 225.6 %all-gather.12.cloned.1.call-start = ((), (), s32[]{:S(2)}) async-start(), calls=%async_computation.4 | async-start | bytes 9191424 | tf_op jit(solution)/shard_map/all_gather | solution.py:67
  39.1 399.7 %all-gather.14.cloned.1.call-start = ((), (), s32[]{:S(2)}) async-start(), calls=%async_computation.5 | async-start | bytes 9191424 | tf_op jit(solution)/shard_map/all_gather | solution.py:68
  39.8 791.4 %reduce-scatter.2.cloned.1.call-start = ((), (), s32[]{:S(2)}) async-start(), calls=%async_computation.2 | async-start | bytes 2785280 | tf_op jit(solution)/shard_map/reduce_scatter | solution.py:81
  490.3 298.7 %copy-start.5 = (bf16[256,1024]{1,0:T(8,128)(2,1)S(1)}, bf16[256,1024]{1,0:T(8,128)(2,1)}, u32[]{:S(2)}) copy-start(bf16[256,1024]{1,0:T(8,128)(2,1)} %param.17) | copy-start | bytes 1572868
  494.2 3.7 copy-start.2
  502.9 3.7 copy-start.2
  511.7 3.7 copy-start.2
  520.5 3.7 copy-start.2
  529.3 3.7 copy-start.2
  538.1 3.7 copy-start.2
  546.8 3.7 copy-start.2
  555.6 3.7 copy-start.2
  564.4 3.7 copy-start.2
  573.2 3.7 copy-start.2
  582.0 3.7 copy-start.2
  590.7 3.7 copy-start.2
  599.5 3.7 copy-start.2
  608.3 3.7 copy-start.2
  617.1 3.7 copy-start.2
  625.9 3.7 copy-start.2
  634.7 3.7 copy-start.2
  643.4 3.7 copy-start.2
  652.2 3.7 copy-start.2
  661.0 3.7 copy-start.2
  669.8 3.7 copy-start.2
  678.6 3.7 copy-start.2
  687.3 3.7 copy-start.2
  696.1 3.7 copy-start.2
  704.9 3.7 copy-start.2
  713.7 3.7 copy-start.2
  722.5 3.7 copy-start.2
  731.3 3.7 copy-start.2
  740.0 3.7 copy-start.2
  748.8 3.7 copy-start.2
  757.6 3.7 copy-start.2
  766.4 3.7 copy-start.2
  775.2 3.7 copy-start.2
  783.9 3.7 copy-start.2
  789.0 2.5 copy-start.7
  789.0 3.4 copy-start.10
  789.0 14.4 %copy-start.6 = (bf16[2,1024,16]{1,2,0:T(8,128)(2,1)S(1)}, bf16[2,1024,16]{1,2,0:T(8,128)(2,1)}, u32[]{:S(2)}) copy-start(bf16[2,1024,16]{1,2,0:T(8,128)(2,1)} %param.21) | copy-start | bytes 196612
  789.1 42.2 %copy-start.3 = (bf16[136,1024]{1,0:T(8,128)(2,1)S(1)}, bf16[136,1024]{1,0:T(8,128)(2,1)}, u32[]{:S(2)}) copy-start(bf16[136,1024]{1,0:T(8,128)(2,1)} %param.12) | copy-start | bytes 835588
  789.1 42.2 %copy-start.8 = (f32[1024]{0:T(1024)S(1)}, f32[1024]{0:T(1024)}, u32[]{:S(2)}) copy-start(f32[1024]{0:T(1024)} %param.14) | copy-start | bytes 12292
  790.9 41.6 %copy-start.9 = (f32[1024]{0:T(1024)S(1)}, f32[1024]{0:T(1024)}, u32[]{:S(2)}) copy-start(f32[1024]{0:T(1024)} %param.15) | copy-start | bytes 12292
  791.0 151.7 %all-gather.10.cloned.1.call-start = ((), (), s32[]{:S(2)}) async-start(), calls=%async_computation.3 | async-start | bytes 20971520 | tf_op jit(solution)/shard_map/all_gather | solution.py:102
  832.5 117.8 %copy-start.4 = (bf16[136,1024]{1,0:T(8,128)(2,1)}, bf16[136,1024]{1,0:T(8,128)(2,1)S(1)}, u32[]{:S(2)}) copy-start(bf16[136,1024]{1,0:T(8,128)(2,1)S(1)} %get-tuple-element.104) | copy-start | bytes 835588
  942.7 8.6 copy-start.1
Sparse Core Ops, SparseCore 0:
  11.1 24.7 all-gather.7
  39.2 197.3 all-gather.11
  238.8 199.9 all-gather.13
  791.1 40.1 reduce-scatter.1
  832.8 109.7 all-gather.9
where the time goes:
time: 962 us; the launch traced here: 958 us
  waiting for transfers between devices  503 us (52%)
  matrix products  264 us (27%)
  local copies, waits for them, and re-layouts  106 us (11%)
  other arithmetic  50.4 us (5%)
  blocking collectives  18.4 us (2%)
  between operations  14 us (1%)
    all_gather x1, waiting for transfers between devices, body(): key_part = lax.all_gather(local_keys, 'seq', axis=0, tiled=True)  197 us
    all_gather x1, waiting for transfers between devices, body(): value_part = lax.all_gather(local_values, 'seq', axis=0, tiled=True)  151 us
    dot_general x34, matrix products, absorb_block(): jnp.einsum('qhd,khd->hqk', query_heads, key_heads, preferred_element_type...  128 us
    dot_general x34, matrix products, absorb_block(): jnp.einsum('hqk,khd->qhd', weights.astype(jnp.bfloat16), value_heads, pre...  123 us
    all_gather x1, waiting for transfers between devices, body(): lax.all_gather(head_w1, 'type', axis=0, tiled=True)  109 us
    unnamed x22, local copies, waits for them, and re-layouts  51.3 us
    reduce_sum x34, other arithmetic, absorb_block(): totals = totals * decay + jnp.sum(weights, axis=-1)  43.5 us
    reshape x1, local copies, waits for them, and re-layouts, body(): key_blocks = key_part.reshape(row_total // 512, 512, local_heads, HD)  25.9 us
  transfers between devices with their start and end apart: 5, of which 5 were waited for; matrix products, arithmetic and copies ran while one was open for 6% of the time, Pallas kernels for 0%

commit v1 on v0

--- a/solution.py
+++ b/solution.py
@@ -65,7 +65,9 @@
     )
     running = initial
     key_part = lax.all_gather(local_keys, "seq", axis=0, tiled=True)
-    value_part = lax.all_gather(local_values, "seq", axis=0, tiled=True)
+    value_part = jnp.concatenate(
+        lax.all_to_all(jnp.stack([local_values] * lax.axis_size("seq")), "seq", 0, 0), axis=0
+    )
     row_total = key_part.shape[0]
     key_blocks = key_part.reshape(row_total // 512, 512, local_heads, HD)
     value_blocks = value_part.reshape(row_total // 512, 512, local_heads, HD)

time: 962 us -> 881 us (0.916)
  waiting for transfers between devices: 503 us -> 412 us
    all_gather x1 -> x0, waiting for transfers between devices: 151 us -> none  [body(): value_part = lax.all_gather(local_values, 'seq', axis=0, tiled=True)]
    all_to_all x0 -> x1, waiting for transfers between devices: none -> 145 us  [body(): lax.all_to_all(jnp.stack([local_values] * lax.axis_size('seq')), 'seq', 0...]
    all_gather x1, waiting for transfers between devices: 197 us -> 112 us  [body(): key_part = lax.all_gather(local_keys, 'seq', axis=0, tiled=True)]
    another operation x1 -> x3, local copies, waits for them, and re-layouts: 0.01 us -> 30.4 us  [the longest x1 25.9 us: body(): value_blocks = value_part.reshape(row_total // 512, 512, local_heads, HD)]
    reshape x1 -> x0, local copies, waits for them, and re-layouts: 25.9 us -> none  [body(): value_blocks = value_part.reshape(row_total // 512, 512, local_heads, HD)]
  transfers between devices with their start and end apart: 5 -> 5, of which waited for: 5 -> 5; matrix products, arithmetic and copies ran while one was open for 6% -> 7% of each run, Pallas kernels for 0% -> 0%
where the time goes in v1:
time: 881 us; the launch traced here: 877 us
  waiting for transfers between devices  412 us (47%)
  matrix products  264 us (30%)
  local copies, waits for them, and re-layouts  111 us (13%)
  other arithmetic  50.4 us (6%)
  blocking collectives  16.9 us (2%)
  between operations  14 us (2%)
    all_to_all x1, waiting for transfers between devices, body(): lax.all_to_all(jnp.stack([local_values] * lax.axis_size('seq')), 'seq', 0...  145 us
    dot_general x34, matrix products, absorb_block(): jnp.einsum('qhd,khd->hqk', query_heads, key_heads, preferred_element_type...  128 us
    dot_general x34, matrix products, absorb_block(): jnp.einsum('hqk,khd->qhd', weights.astype(jnp.bfloat16), value_heads, pre...  123 us
    all_gather x1, waiting for transfers between devices, body(): key_part = lax.all_gather(local_keys, 'seq', axis=0, tiled=True)  112 us
    all_gather x1, waiting for transfers between devices, body(): lax.all_gather(head_w1, 'type', axis=0, tiled=True)  109 us
    unnamed x22, local copies, waits for them, and re-layouts  51.3 us
    reduce_sum x34, other arithmetic, absorb_block(): totals = totals * decay + jnp.sum(weights, axis=-1)  43.5 us
    another operation x1, local copies, waits for them, and re-layouts, body(): value_blocks = value_part.reshape(row_total // 512, 512, local_heads, HD)  25.9 us
  transfers between devices with their start and end apart: 5, of which 5 were waited for; matrix products, arithmetic and copies ran while one was open for 7% of the time, Pallas kernels for 0%

profile of v1, /device:TPU:1, one launch (start us, length us, event | category | flops | bytes accessed | tf_op | source)
XLA Modules:
  0.0 877.3 jit_solution(10209492818713163507)
XLA Ops:
  11.1 24.9 %all-gather.6.cloned.1.call-done = bf16[544,1024]{1,0:T(8,128)(2,1)} async-done(((bf16[136,1024]{1,0:T(8,128)(2,1)}), bf16[544,1024]{1,0:T(8,128)(2,1)}) %all-gather.6.cloned.1.call-update) | async-done | bytes 1114128 | tf_op jit(solution)/shard_map/all_gather | solution.py:50
  39.0 4.4 stack.3
  43.4 7.1 all-to-all-start
  50.8 145.0 %all-to-all-done = bf16[32,544,256]{2,1,0:T(8,128)(2,1)} async-done(((bf16[32,544,256]{2,1,0:T(8,128)(2,1)}), bf16[32,544,256]{2,1,0:T(8,128)(2,1)}, u32[]{:S(2)}, u32[]{:S(2)}) %all-to-all-start) | async-done | bytes 8912928 | tf_op jit(solution)/shard_map/all_to_all | solution.py:69
  195.8 25.9 %reshape.73 = bf16[34,512,4,64]{3,2,1,0:T(4,128)(2,1)} reshape(bf16[32,544,256]{2,1,0:T(8,128)(2,1)} %all-to-all-done) | data formatting | bytes 17825792 | tf_op jit(solution)/shard_map/reshape;reshape | solution.py:73
  221.8 25.6 %copy.24 = bf16[34,512,4,64]{1,3,2,0:T(8,128)(2,1)} copy(bf16[34,512,4,64]{3,2,1,0:T(4,128)(2,1)} %reshape.73) | data formatting | bytes 17825792
  247.4 111.7 %all-gather.10.cloned.1.call-done = bf16[1,17408,256]{2,1,0:T(8,128)(2,1)} async-done(((bf16[1,544,256]{2,1,0:T(8,128)(2,1)}), bf16[1,17408,256]{2,1,0:T(8,128)(2,1)}) %all-gather.10.cloned.1.call-update) | async-done | bytes 8912912 | tf_op jit(solution)/shard_map/all_gather | solution.py:67
  359.1 25.9 %reshape.72 = bf16[34,512,4,64]{3,2,1,0:T(4,128)(2,1)} reshape(bf16[1,17408,256]{2,1,0:T(8,128)(2,1)} %all-gather.10.cloned.1.call-done) | data formatting | bytes 17825792 | tf_op jit(solution)/shard_map/reshape | solution.py:72
  385.0 25.6 %copy.23 = bf16[34,512,4,64]{1,3,2,0:T(8,128)(2,1)} copy(bf16[34,512,4,64]{3,2,1,0:T(4,128)(2,1)} %reshape.72) | data formatting | bytes 17825792
  410.6 298.8 %while.15 = (s32[]{:T(128)}, f32[4,544]{1,0:T(4,128)S(1)}, f32[4,544]{1,0:T(4,128)S(1)}, f32[544,4,64]{0,2,1:T(8,128)S(1)}, bf16[34,512,4,64]{1,3,2,0:T(8,128)(2...) while((s32[]{:T(128)}, f32[4,544]{1,0:T(4,128)S(1)}, ...), condition=%wide.region_4.5_spmd.clone, body=%wide.region_1.4_spmd.clone.sunk | while | flops 294556416 | bytes 33252484 | solution.py:78
  410.6 3.8 bitcast_reduce_fusion.2
  419.4 3.8 bitcast_reduce_fusion.2
  423.2 3.6 fusion.82
  428.2 3.8 bitcast_reduce_fusion.2
  432.0 3.6 fusion.82
  437.0 3.8 bitcast_reduce_fusion.2
  445.8 3.8 bitcast_reduce_fusion.2
  449.6 3.6 fusion.82
  454.6 3.8 bitcast_reduce_fusion.2
  458.4 3.6 fusion.82
  463.4 3.8 bitcast_reduce_fusion.2
  472.2 3.8 bitcast_reduce_fusion.2
  475.9 3.6 fusion.82
  480.9 3.8 bitcast_reduce_fusion.2
  484.7 3.6 fusion.82
  489.7 3.8 bitcast_reduce_fusion.2
  498.5 3.8 bitcast_reduce_fusion.2
  502.3 3.6 fusion.82
  507.3 3.8 bitcast_reduce_fusion.2
  516.1 3.8 bitcast_reduce_fusion.2
  524.9 3.8 bitcast_reduce_fusion.2
  528.7 3.6 fusion.82
  533.7 3.8 bitcast_reduce_fusion.2
  537.4 3.6 fusion.82
  542.4 3.8 bitcast_reduce_fusion.2
  551.2 3.8 bitcast_reduce_fusion.2
  555.0 3.6 fusion.82
  560.0 3.8 bitcast_reduce_fusion.2
  568.8 3.8 bitcast_reduce_fusion.2
  577.6 3.8 bitcast_reduce_fusion.2
  581.4 3.6 fusion.82
  586.4 3.8 bitcast_reduce_fusion.2
  595.2 3.8 bitcast_reduce_fusion.2
  603.9 3.8 bitcast_reduce_fusion.2
  607.7 3.6 fusion.82
  612.7 3.8 bitcast_reduce_fusion.2
  621.5 3.8 bitcast_reduce_fusion.2
  630.3 3.8 bitcast_reduce_fusion.2
  634.1 3.6 fusion.82
  639.1 3.8 bitcast_reduce_fusion.2
  647.9 3.8 bitcast_reduce_fusion.2
  656.7 3.8 bitcast_reduce_fusion.2
  660.5 3.6 fusion.82
  665.4 3.8 bitcast_reduce_fusion.2
  674.2 3.8 bitcast_reduce_fusion.2
  683.0 3.8 bitcast_reduce_fusion.2
  686.8 3.6 fusion.82
  691.8 3.8 bitcast_reduce_fusion.2
  700.6 3.8 bitcast_reduce_fusion.2
  712.8 9.5 %all-gather.1 = bf16[4,2,1024]{2,1,0:T(2,128)(2,1)S(1)} all-gather(bf16[1,2,1024]{2,1,0:T(2,128)(2,1)S(1)} %bitcast.85), channel_id=1, replica_groups=mesh['seq'=32,'type'=4] {'type'}, dimensions={0}, use_global_device_ids=true | all-gather | bytes 20480 | tf_op jit(solution)/shard_map/all_gather | solution.py:105
  722.4 7.4 all_gather.19
  729.9 20.7 %reduce-scatter.2.cloned.1.call-done = f32[136,1024]{1,0:T(8,128)} async-done(((f32[544,1024]{1,0:T(8,128)}), f32[136,1024]{1,0:T(8,128)}) %reduce-scatter.2.cloned.1.call-update) | async-done | bytes 557072 | tf_op jit(solution)/shard_map/reduce_scatter | solution.py:83
  752.6 109.4 %all-gather.8.cloned.1.call-done = bf16[8,1024,1024]{2,1,0:T(8,128)(2,1)} async-done(((bf16[2,1024,1024]{2,1,0:T(8,128)(2,1)}), bf16[8,1024,1024]{2,1,0:T(8,128)(2,1)}) %all-gather.8.cloned.1.call-update) | async-done | bytes 16777232 | tf_op jit(solution)/shard_map/all_gather | solution.py:104
  862.1 7.6 fusion.32
  (281 shorter events, 128.5 us)
Async XLA Ops:
  7.2 28.8 %copy-start = (bf16[3,1024,256]{2,1,0:T(8,128)(2,1)S(1)}, bf16[3,1024,256]{2,1,0:T(8,128)(2,1)}, u32[]{:S(2)}) copy-start(bf16[3,1024,256]{2,1,0:T(8,128)(2,1)} %param.16) | copy-start | bytes 4718596
  7.2 28.7 %all-gather.6.cloned.1.call-start = ((), (), s32[]{:S(2)}) async-start(), calls=%async_computation.2 | async-start | bytes 1392640 | tf_op jit(solution)/shard_map/all_gather | solution.py:50
  11.0 348.0 %all-gather.10.cloned.1.call-start = ((), (), s32[]{:S(2)}) async-start(), calls=%async_computation.5 | async-start | bytes 9191424 | tf_op jit(solution)/shard_map/all_gather | solution.py:67
  43.4 152.4 %all-to-all-start = ((bf16[32,544,256]{2,1,0:T(8,128)(2,1)}), bf16[32,544,256]{2,1,0:T(8,128)(2,1)}, u32[]{:S(2)}, u32[]{:S(2)}) async-start(bf16[32,544,256]{2,1,0:T(8,128)(2,1)} %stack.3), calls=%async_computation | async-start | bytes 17825792 | tf_op jit(solution)/shard_map/all_to_all | solution.py:69
  50.5 700.1 %reduce-scatter.2.cloned.1.call-start = ((), (), s32[]{:S(2)}) async-start(), calls=%async_computation.3 | async-start | bytes 2785280 | tf_op jit(solution)/shard_map/reduce_scatter | solution.py:83
  410.6 298.8 %copy-start.5 = (bf16[256,1024]{1,0:T(8,128)(2,1)S(1)}, bf16[256,1024]{1,0:T(8,128)(2,1)}, u32[]{:S(2)}) copy-start(bf16[256,1024]{1,0:T(8,128)(2,1)} %param.17) | copy-start | bytes 1572868
  414.4 3.7 copy-start.2
  423.2 3.7 copy-start.2
  432.0 3.7 copy-start.2
  440.8 3.7 copy-start.2
  449.6 3.7 copy-start.2
  458.4 3.7 copy-start.2
  467.1 3.7 copy-start.2
  475.9 3.7 copy-start.2
  484.7 3.7 copy-start.2
  493.5 3.7 copy-start.2
  502.3 3.7 copy-start.2
  511.1 3.7 copy-start.2
  519.9 3.7 copy-start.2
  528.6 3.7 copy-start.2
  537.4 3.7 copy-start.2
  546.2 3.7 copy-start.2
  555.0 3.7 copy-start.2
  563.8 3.7 copy-start.2
  572.6 3.7 copy-start.2
  581.4 3.7 copy-start.2
  590.1 3.7 copy-start.2
  598.9 3.7 copy-start.2
  607.7 3.7 copy-start.2
  616.5 3.7 copy-start.2
  625.3 3.7 copy-start.2
  634.1 3.7 copy-start.2
  642.9 3.7 copy-start.2
  651.6 3.7 copy-start.2
  660.4 3.7 copy-start.2
  669.2 3.7 copy-start.2
  678.0 3.7 copy-start.2
  686.8 3.7 copy-start.2
  695.6 3.7 copy-start.2
  704.4 3.7 copy-start.2
  709.4 2.5 copy-start.7
  709.5 3.4 copy-start.10
  709.5 12.9 %copy-start.6 = (bf16[2,1024,16]{1,2,0:T(8,128)(2,1)S(1)}, bf16[2,1024,16]{1,2,0:T(8,128)(2,1)}, u32[]{:S(2)}) copy-start(bf16[2,1024,16]{1,2,0:T(8,128)(2,1)} %param.21) | copy-start | bytes 196612
  709.5 41.1 %copy-start.3 = (bf16[136,1024]{1,0:T(8,128)(2,1)S(1)}, bf16[136,1024]{1,0:T(8,128)(2,1)}, u32[]{:S(2)}) copy-start(bf16[136,1024]{1,0:T(8,128)(2,1)} %param.12) | copy-start | bytes 835588
  709.5 41.1 %copy-start.8 = (f32[1024]{0:T(1024)S(1)}, f32[1024]{0:T(1024)}, u32[]{:S(2)}) copy-start(f32[1024]{0:T(1024)} %param.14) | copy-start | bytes 12292
  711.4 40.5 %copy-start.9 = (f32[1024]{0:T(1024)S(1)}, f32[1024]{0:T(1024)}, u32[]{:S(2)}) copy-start(f32[1024]{0:T(1024)} %param.15) | copy-start | bytes 12292
  711.4 150.7 %all-gather.8.cloned.1.call-start = ((), (), s32[]{:S(2)}) async-start(), calls=%async_computation.4 | async-start | bytes 20971520 | tf_op jit(solution)/shard_map/all_gather | solution.py:104
  751.9 117.8 %copy-start.4 = (bf16[136,1024]{1,0:T(8,128)(2,1)}, bf16[136,1024]{1,0:T(8,128)(2,1)S(1)}, u32[]{:S(2)}) copy-start(bf16[136,1024]{1,0:T(8,128)(2,1)S(1)} %get-tuple-element.104) | copy-start | bytes 835588
  862.1 8.6 copy-start.1
Sparse Core Ops, SparseCore 0:
  11.1 24.7 all-gather.5
  39.1 319.8 all-gather.9
  711.5 39.0 reduce-scatter.1
  752.2 109.7 all-gather.7
